TPU v7x, 512 devices: a whole 4x4x16 slice. The times are simulated.
512 devices in a mesh: seq: 32 (over z, core), tensor: 16 (over y, x).
Axes of the slice: x: 4, y: 4, z: 16, core: 2. Of those that a mesh axis runs over, the one named last changes fastest.
Arguments:
- hidden: bfloat16 [4, 64, 5120], P(None, None, 'seq'), may hold values from -400 to 400
- norm_gain: bfloat16 [5120], P('seq'), may hold values from 0.099609375 to 1.8984375
- w_qkv: bfloat16 [5120, 7168], P('seq', 'tensor'), may hold values from -0.078125 to 0.078125
- b_qkv: bfloat16 [7168], P('tensor'), may hold values from -3 to 3
- w_out: bfloat16 [5120, 5120], P('tensor', 'seq'), may hold values from -0.078125 to 0.078125
- prefix_key_cache: bfloat16 [16, 12288, 1024], P('tensor', 'seq'), may hold values from -140 to 140
- prefix_value_cache: bfloat16 [16, 12288, 1024], P('tensor', 'seq'), may hold values from -6 to 6
- suffix_key_cache: bfloat16 [64, 4096, 1024], P('tensor', 'seq'), may hold values from -8 to 8
- suffix_value_cache: bfloat16 [64, 4096, 1024], P('tensor', 'seq'), may hold values from -6 to 6
- prefix_lens: int32 [16], P('tensor'), may hold values from 1 to 12288, as said below
- suffix_lens: int32 [64], P('tensor'), may hold values from 0 to 4096, as said below
Outputs:
- attn_out: float32 [4, 64, 5120], P(None, 'tensor', 'seq')
- new_keys: float32 [64, 4, 1024], P('tensor')
- new_values: float32 [64, 4, 1024], P('tensor')
Inputs may be any that keep to these rules, and one draw needn't show every extreme that they name: `prefix_lens`: some group has exactly 12288 live slots and some exactly one. `suffix_lens`: some request has exactly 4096 live slots and some none.
All inputs are finite; a program needn't handle non-finite values.
Results may differ from a plain program's by a relative error of at most 0.012.
The roundings to bfloat16 on the way count: a program that leaves them out, or rounds other values in their place, can miss the bound.
Values may be sent and summed in bfloat16 or wider, within the bound.
No kernel may reach another device: no remote copies, remote signals or barrier semaphores. Data moves between devices by JAX's collectives and lax.ppermute only.
A program may use at most 64 MiB of HBM per device.

v0:
```python
import jax
import jax.numpy as jnp
from jax import lax
from jax.sharding import PartitionSpec as P

D = 5120
QUERY_HEADS = 40
KEY_HEADS = 8
HEAD_SIZE = 128
KEY_COLUMNS = 1024
SEQ = ("z", "core")
epsilon = 1e-06
masked_fill = -1e30


def apply_rotary(values, token_positions):
    half = values.shape[-1] // 2
    freq = jnp.exp(
        -(jnp.arange(half, dtype=jnp.float32) * (2.0 / values.shape[-1]))
        * jnp.log(jnp.float32(1000000.0))
    )
    angles = token_positions[..., None, None] * freq
    cosine = jnp.cos(angles)
    sine = jnp.sin(angles)
    left = values[..., :half]
    right = values[..., half:]
    return jnp.concatenate([left * cosine - right * sine, right * cosine + left * sine], axis=-1)


def body(
    hidden,
    norm_gain,
    w_qkv,
    b_qkv,
    w_out,
    prefix_key_cache,
    prefix_value_cache,
    suffix_key_cache,
    suffix_value_cache,
    prefix_lens,
    suffix_lens,
):
    seq_count = lax.axis_size(SEQ)
    tensor_count = lax.axis_size("tensor")
    steps = hidden.shape[0]
    request_total = hidden.shape[1]
    requests = suffix_lens.shape[0]
    columns = w_qkv.shape[1]
    prefix_count = prefix_key_cache.shape[1]
    suffix_count = suffix_key_cache.shape[1]
    query_group_width = QUERY_HEADS // KEY_HEADS
    query_width = QUERY_HEADS * HEAD_SIZE
    query_rows = steps * query_group_width
    scale = float(HEAD_SIZE) ** (-0.5)
    seq_index = lax.axis_index(SEQ)
    w_out_cols = lax.all_gather(w_out, "tensor", axis=0, tiled=True)
    xf = hidden.astype(jnp.float32)
    local_squares = jnp.sum(xf * xf, axis=2)
    squares = jnp.sum(
        lax.all_to_all(
            jnp.broadcast_to(local_squares[None], (seq_count,) + local_squares.shape),
            SEQ,
            0,
            0,
            tiled=True,
        ),
        axis=0,
    )
    normed = (
        xf * lax.rsqrt(squares / D + epsilon)[..., None] * norm_gain.astype(jnp.float32)
    ).astype(jnp.bfloat16)
    partial_value = jnp.einsum("sbd,dc->sbc", normed, w_qkv, preferred_element_type=jnp.float32)
    halves = seq_count // (steps * requests)
    half_width = columns // halves
    groups = request_total // requests
    core = lax.axis_index("core")
    plane_count = seq_count // halves
    by_half = partial_value.reshape(steps, groups, requests, halves, half_width)
    keep = lax.dynamic_index_in_dim(by_half, core, axis=3, keepdims=False)
    send = lax.dynamic_index_in_dim(by_half, 1 - core, axis=3, keepdims=False)
    pair_sum = keep + lax.ppermute(send, "core", [(0, 1), (1, 0)])
    chunks = pair_sum.transpose(0, 2, 1, 3).reshape(plane_count, groups, half_width)
    reduced = jnp.sum(lax.all_to_all(chunks, "z", 0, 0, tiled=True), axis=0)
    bias = lax.dynamic_slice_in_dim(
        b_qkv.astype(jnp.float32), seq_index % halves * half_width, half_width
    )
    reduced = reduced + bias[None, :]
    owned_rows = lax.all_to_all(reduced, "tensor", 0, 0, tiled=True)
    gathered = lax.all_gather(owned_rows, SEQ, axis=0, tiled=False)
    combined_output = (
        gathered.reshape(steps, requests, halves, tensor_count, half_width)
        .transpose(0, 1, 3, 2, 4)
        .reshape(steps, requests, tensor_count * columns)
    )
    token_positions = (
        (prefix_lens[0] + suffix_lens)[None, :] + jnp.arange(steps, dtype=jnp.int32)[:, None]
    ).astype(jnp.float32)
    query_matrix = apply_rotary(
        combined_output[..., :query_width].reshape(steps, requests, QUERY_HEADS, HEAD_SIZE),
        token_positions,
    ).astype(jnp.bfloat16)
    keys_float = apply_rotary(
        combined_output[..., query_width : query_width + KEY_COLUMNS].reshape(
            steps, requests, KEY_HEADS, HEAD_SIZE
        ),
        token_positions,
    )
    values_float = combined_output[..., query_width + KEY_COLUMNS :].reshape(
        steps, requests, KEY_HEADS, HEAD_SIZE
    )
    current_keys = keys_float.astype(jnp.bfloat16)
    current_values = values_float.astype(jnp.bfloat16)
    new_keys = keys_float.reshape(steps, requests, KEY_COLUMNS).transpose(1, 0, 2)
    new_values = values_float.reshape(steps, requests, KEY_COLUMNS).transpose(1, 0, 2)
    query_by_group = (
        query_matrix.reshape(steps, requests, KEY_HEADS, query_group_width, HEAD_SIZE)
        .transpose(1, 2, 0, 3, 4)
        .reshape(requests, KEY_HEADS, query_rows, HEAD_SIZE)
    )
    prefix_key_block = prefix_key_cache[0].reshape(prefix_count, KEY_HEADS, HEAD_SIZE)
    prefix_value_block = prefix_value_cache[0].reshape(prefix_count, KEY_HEADS, HEAD_SIZE)
    suffix_key_block = suffix_key_cache.reshape(requests, suffix_count, KEY_HEADS, HEAD_SIZE)
    suffix_value_block = suffix_value_cache.reshape(requests, suffix_count, KEY_HEADS, HEAD_SIZE)
    score_pre = (
        jnp.einsum(
            "rhqd,phd->rhqp", query_by_group, prefix_key_block, preferred_element_type=jnp.float32
        )
        * scale
    )
    score_suf = (
        jnp.einsum(
            "rhqd,rshd->rhqs", query_by_group, suffix_key_block, preferred_element_type=jnp.float32
        )
        * scale
    )
    pre_mask = (
        seq_index * prefix_count + jnp.arange(prefix_count, dtype=jnp.int32) < prefix_lens[0]
    )[None, None, None, :]
    suf_mask = (
        (seq_index * suffix_count + jnp.arange(suffix_count, dtype=jnp.int32))[None, :]
        < suffix_lens[:, None]
    )[:, None, None, :]
    fill_pre = jnp.where(pre_mask, score_pre, masked_fill)
    fill_suf = jnp.where(suf_mask, score_suf, masked_fill)
    local_max = jnp.maximum(jnp.max(fill_pre, axis=3), jnp.max(fill_suf, axis=3))
    prob_pre = jnp.where(pre_mask, jnp.exp(fill_pre - local_max[..., None]), 0.0)
    prob_suf = jnp.where(suf_mask, jnp.exp(fill_suf - local_max[..., None]), 0.0)
    local_weight = jnp.sum(prob_pre, axis=3) + jnp.sum(prob_suf, axis=3)
    local_acc = jnp.einsum(
        "rhqp,phd->rhqd",
        prob_pre.astype(jnp.bfloat16),
        prefix_value_block,
        preferred_element_type=jnp.float32,
    )
    local_acc = local_acc + jnp.einsum(
        "rhqs,rshd->rhqd",
        prob_suf.astype(jnp.bfloat16),
        suffix_value_block,
        preferred_element_type=jnp.float32,
    )
    fresh_k = current_keys.transpose(1, 2, 0, 3)
    fresh_v = current_values.transpose(1, 2, 0, 3)
    score_new = (
        jnp.einsum("rhqd,rhid->rhqi", query_by_group, fresh_k, preferred_element_type=jnp.float32)
        * scale
    )
    new_mask = (
        (jnp.arange(query_rows, dtype=jnp.int32) // query_group_width)[:, None]
        >= jnp.arange(steps, dtype=jnp.int32)[None, :]
    )[None, None]
    fill_new = jnp.where(new_mask, score_new, masked_fill)
    new_max = jnp.max(fill_new, axis=3)
    prob_new = jnp.where(new_mask, jnp.exp(fill_new - new_max[..., None]), 0.0)
    new_weight = jnp.sum(prob_new, axis=3)
    new_acc = jnp.einsum(
        "rhqi,rhid->rhqd",
        prob_new.astype(jnp.bfloat16),
        fresh_v,
        preferred_element_type=jnp.float32,
    )
    lane_pad = ((0, 0), (0, 0), (0, HEAD_SIZE - query_rows))
    packed = jnp.concatenate(
        [
            local_acc,
            jnp.pad(local_max, lane_pad)[:, :, None, :],
            jnp.pad(local_weight, lane_pad)[:, :, None, :],
        ],
        axis=2,
    ).reshape(requests, KEY_HEADS // 2, 2, query_rows + 2, HEAD_SIZE)
    keep = lax.dynamic_index_in_dim(packed, core, axis=2, keepdims=False)
    came = lax.ppermute(
        lax.dynamic_index_in_dim(packed, 1 - core, axis=2, keepdims=False), "core", [(0, 1), (1, 0)]
    )
    keep_max = keep[..., query_rows, :query_rows]
    came_max = came[..., query_rows, :query_rows]
    pair_max = jnp.maximum(keep_max, came_max)
    keep_factor = jnp.exp(keep_max - pair_max)
    came_factor = jnp.exp(came_max - pair_max)
    pair_weight = (
        keep[..., query_rows + 1, :query_rows] * keep_factor
        + came[..., query_rows + 1, :query_rows] * came_factor
    )
    pair_acc = (
        keep[..., :query_rows, :] * keep_factor[..., None]
        + came[..., :query_rows, :] * came_factor[..., None]
    )
    pad_rows = ((0, 0), (0, 0), (0, HEAD_SIZE - query_rows))
    pair_packed = jnp.concatenate(
        [
            pair_acc,
            jnp.pad(pair_max, pad_rows)[:, :, None, :],
            jnp.pad(pair_weight, pad_rows)[:, :, None, :],
        ],
        axis=2,
    ).reshape(seq_count // 2, query_rows + 2, HEAD_SIZE)
    arrived = lax.all_to_all(pair_packed, "z", 0, 0, tiled=True)
    w_out_cols, arrived = lax.optimization_barrier((w_out_cols, arrived))
    part_acc = arrived[:, :query_rows, :]
    part_max = arrived[:, query_rows, :query_rows]
    part_weight = arrived[:, query_rows + 1, :query_rows]
    global_max = jnp.max(part_max, axis=0)
    factor = jnp.exp(part_max - global_max[None])
    global_weight = jnp.sum(part_weight * factor, axis=0)
    global_acc = jnp.sum(part_acc * factor[..., None], axis=0)
    mine_r = seq_index // KEY_HEADS
    mine_h = seq_index % KEY_HEADS
    own_new_max = new_max[mine_r, mine_h]
    own_new_weight = new_weight[mine_r, mine_h]
    own_new_acc = new_acc[mine_r, mine_h]
    top = jnp.maximum(global_max, own_new_max)
    factor_old = jnp.exp(global_max - top)
    factor_new = jnp.exp(own_new_max - top)
    total = global_weight * factor_old + own_new_weight * factor_new
    summed = global_acc * factor_old[..., None] + own_new_acc * factor_new[..., None]
    attention_slice = (summed / total[..., None]).astype(jnp.bfloat16)
    attention_all = lax.all_to_all(
        jnp.broadcast_to(attention_slice[None], (seq_count,) + attention_slice.shape),
        SEQ,
        0,
        0,
        tiled=True,
    )
    heads_local = (
        attention_all.reshape(requests, KEY_HEADS, steps, query_group_width, HEAD_SIZE)
        .transpose(2, 0, 1, 3, 4)
        .reshape(steps, requests, query_width)
    )
    owned = jnp.einsum("sbc,cd->sbd", heads_local, w_out_cols, preferred_element_type=jnp.float32)
    return (owned, new_keys, new_values)


def solution(mesh):
    placed = (
        P(None, None, SEQ),
        P(SEQ),
        P(SEQ, "tensor"),
        P("tensor"),
        P("tensor", SEQ),
        P("tensor", SEQ, None),
        P("tensor", SEQ, None),
        P("tensor", SEQ, None),
        P("tensor", SEQ, None),
        P("tensor"),
        P("tensor"),
    )
    planes = jax.sharding.Mesh(
        mesh.devices.reshape(-1, 2, mesh.devices.shape[1]), ("z", "core", "tensor")
    )
    return jax.shard_map(
        body,
        mesh=planes,
        in_specs=placed,
        out_specs=(
            P(None, "tensor", ("z", "core")),
            P("tensor", None, None),
            P("tensor", None, None),
        ),
        check_vma=False,
    )
```

profile of v0, /device:TPU:1, one launch (start us, length us, event | category | flops | bytes accessed | tf_op | source)
XLA Modules:
  0.0 182.2 jit_solution(754688764741654744)
XLA Ops:
  7.2 1.1 fusion.20
  9.0 16.7 %all-to-all-start = ((f32[32,1,256]{2,1,0:T(1,128)}), f32[32,1,256]{2,1,0:T(1,128)S(1)}, u32[]{:S(2)}, u32[]{:S(2)}) async-start(f32[32,1,256]{2,1,0:T(1,128)} %reshape.346), calls=%async_computation | async-start | bytes 65536 | tf_op jit(solution)/shard_map/all_to_all | solution.py:60
  27.2 10.7 %all-to-all-done = f32[32,1,256]{2,1,0:T(1,128)S(1)} async-done(((f32[32,1,256]{2,1,0:T(1,128)}), f32[32,1,256]{2,1,0:T(1,128)S(1)}, u32[]{:S(2)}, u32[]{:S(2)}) %all-to-all-start) | async-done | bytes 32800 | tf_op jit(solution)/shard_map/all_to_all | solution.py:60
  39.3 1.2 fusion.28
  41.6 3.2 %collective-permute-start = (f32[4,16,4,224]{3,1,2,0:T(8,128)S(1)}, f32[4,16,4,224]{3,1,2,0:T(8,128)S(1)}, u32[]{:S(2)}, u32[]{:S(2)}) collective-permute-start(f32[4,16,4,224]{3,1,2,0:T(8,128)S(1)} %bitcast.160), channel_id=1, source_target_pairs={{0,16},{16,0},{1,17},{17,1},{2,18},{18,2},{3,19},{19,3},{4,20},{20... | collective-permute-start | bytes 688136 | tf_op jit(solution)/shard_map/ppermute | solution.py:81
  45.9 0.8 bitcast_add_fusion
  46.7 3.5 %all-to-all-start.1 = ((f32[16,16,224]{2,1,0:T(8,128)}), f32[16,16,224]{2,1,0:T(8,128)S(1)}, u32[]{:S(2)}, u32[]{:S(2)}) async-start(f32[16,16,224]{2,1,0:T(8,128)} %bitcast.6), calls=%async_computation.1 | async-start | bytes 524288 | tf_op jit(solution)/shard_map/all_to_all | solution.py:83
  50.5 14.1 %all-to-all-done.1 = f32[16,16,224]{2,1,0:T(8,128)S(1)} async-done(((f32[16,16,224]{2,1,0:T(8,128)}), f32[16,16,224]{2,1,0:T(8,128)S(1)}, u32[]{:S(2)}, u32[]{:S(2)}) %all-to-all-start.1) | async-done | bytes 229408 | tf_op jit(solution)/shard_map/all_to_all | solution.py:83
  65.2 6.8 %all-to-all-start.2 = ((f32[16,1,224]{2,1,0:T(1,128)}), f32[16,1,224]{2,1,0:T(1,128)S(1)}, u32[]{:S(2)}, u32[]{:S(2)}) async-start(f32[16,1,224]{2,1,0:T(1,128)} %reshape_add_fusion), calls=%async_computation.2 | async-start | bytes 32768 | tf_op jit(solution)/shard_map/all_to_all | solution.py:88
  72.2 2.2 %copy.290 = bf16[48,8,8,128]{3,2,1,0:T(8,128)(2,1)} copy(bf16[48,8,8,128]{3,1,2,0:T(8,128)(2,1)} %bitcast.154) | data formatting | bytes 1572864
  74.4 4.0 %all-to-all-done.2 = f32[16,1,224]{2,1,0:T(1,128)S(1)} async-done(((f32[16,1,224]{2,1,0:T(1,128)}), f32[16,1,224]{2,1,0:T(1,128)S(1)}, u32[]{:S(2)}, u32[]{:S(2)}) %all-to-all-start.2) | async-done | bytes 14368 | tf_op jit(solution)/shard_map/all_to_all | solution.py:88
  78.4 38.2 %all-gather = f32[512,1,224]{2,0,1:T(8,128)S(1)} all-gather(f32[16,1,224]{2,0,1:T(8,128)S(1)} %copy.232), channel_id=2, replica_groups=mesh['z'=16,'core'=2,'tensor'=16] {'z','core'}, dimensions={0}, use_global_device_ids=true | all-gather | bytes 473088 | tf_op jit(solution)/shard_map/all_gather | solution.py:89
  117.1 0.8 reshape.329
  122.3 2.1 %collective-permute-start.1 = (f32[4,4,22,128]{3,1,0,2:T(4,128)S(1)}, f32[4,4,22,128]{3,1,0,2:T(4,128)S(1)}, u32[]{:S(2)}, u32[]{:S(2)}) collective-permute-start(f32[4,4,22,128]{3,1,0,2:T(4,128)S(1)} %copy.256), channel_id=1, source_target_pairs={{0,16},{16,0},{1,17},{17,1},{2,18},{18,2},{3,19},{19,3},{4,20},{20... | collective-permute-start | bytes 540680 | tf_op jit(solution)/shard_map/ppermute | solution.py:191
  124.5 1.1 collective-permute-done.1
  126.9 4.2 %all-to-all-start.3 = ((f32[16,22,128]{2,1,0:T(8,128)}), f32[16,22,128]{2,1,0:T(8,128)S(1)}, u32[]{:S(2)}, u32[]{:S(2)}) async-start(f32[16,22,128]{2,1,0:T(8,128)} %copy.259), calls=%async_computation.3 | async-start | bytes 393216 | tf_op jit(solution)/shard_map/all_to_all | solution.py:216
  131.6 1.1 fusion.35
  132.8 2.2 %copy.228 = bf16[16,320,160]{1,0,2:T(8,128)(2,1)S(1)} copy(bf16[16,320,160]{1,2,0:T(8,128)(2,1)} %all-gather.4.cloned.1.call-done) | data formatting | bytes 3276800 | tf_op jit(solution)/shard_map/all_gather | solution.py:56
  135.0 2.5 %reshape.341 = bf16[5120,160]{0,1:T(8,128)(2,1)} reshape(bf16[16,320,160]{1,0,2:T(8,128)(2,1)S(1)} %copy.228) | data formatting | bytes 3276800 | tf_op jit(solution)/shard_map/optimization_barrier | solution.py:217
  137.5 6.8 %all-to-all-done.3 = f32[16,22,128]{2,1,0:T(8,128)S(1)} async-done(((f32[16,22,128]{2,1,0:T(8,128)}), f32[16,22,128]{2,1,0:T(8,128)S(1)}, u32[]{:S(2)}, u32[]{:S(2)}) %all-to-all-start.3) | async-done | bytes 180256 | tf_op jit(solution)/shard_map/all_to_all | solution.py:216
  144.6 0.9 fusion.46
  146.2 9.2 %all-to-all-start.4 = ((bf16[32,20,128]{2,1,0:T(8,128)(2,1)}), bf16[32,20,128]{2,1,0:T(8,128)(2,1)S(1)}, u32[]{:S(2)}, u32[]{:S(2)}) async-start(bf16[32,20,128]{2,1,0:T(8,128)(2,1)} %broadcast_in_dim.111), calls=%async_computation.4 | async-start | bytes 393216 | tf_op jit(solution)/shard_map/all_to_all | solution.py:236
  156.7 17.2 %all-to-all-done.4 = bf16[32,20,128]{2,1,0:T(8,128)(2,1)S(1)} async-done(((bf16[32,20,128]{2,1,0:T(8,128)(2,1)}), bf16[32,20,128]{2,1,0:T(8,128)(2,1)S(1)}, u32[]{:S(2)}, u32[]{:S(2)}) %all-to-all-start.4) | async-done | bytes 163872 | tf_op jit(solution)/shard_map/all_to_all | solution.py:236
  174.2 1.2 fusion
  (94 shorter events, 15.2 us)
Async XLA Ops:
  7.2 112.0 %copy-start = (bf16[4,128,1024]{2,1,0:T(8,128)(2,1)S(1)}, bf16[4,128,1024]{2,1,0:T(8,128)(2,1)}, u32[]{:S(2)}) copy-start(bf16[4,128,1024]{2,1,0:T(8,128)(2,1)} %param.18) | copy-start | bytes 3145732
  9.0 28.9 %all-to-all-start = ((f32[32,1,256]{2,1,0:T(1,128)}), f32[32,1,256]{2,1,0:T(1,128)S(1)}, u32[]{:S(2)}, u32[]{:S(2)}) async-start(f32[32,1,256]{2,1,0:T(1,128)} %reshape.346), calls=%async_computation | async-start | bytes 65536 | tf_op jit(solution)/shard_map/all_to_all | solution.py:60
  25.8 107.0 %all-gather.4.cloned.1.call-start = ((), (), s32[]{:S(2)}) async-start(), calls=%async_computation.5 | async-start | bytes 2088960 | tf_op jit(solution)/shard_map/all_gather | solution.py:56
  40.5 4.9 %copy-start.5 = (bf16[448]{0:T(512)(128)(2,1)S(1)}, bf16[448]{0:T(512)(128)(2,1)}, u32[]{:S(2)}) copy-start(bf16[448]{0:T(512)(128)(2,1)} %param.14) | copy-start | bytes 2692
  41.5 8.7 %copy-start.6 = (s32[4]{0:T(128)S(1)}, s32[4]{0:T(128)}, u32[]{:S(2)}) copy-start(s32[4]{0:T(128)} %param.21) | copy-start | bytes 52
  41.5 30.5 %copy-start.3 = (bf16[1,384,1024]{2,1,0:T(8,128)(2,1)S(1)}, bf16[1,384,1024]{2,1,0:T(8,128)(2,1)}, u32[]{:S(2)}) copy-start(bf16[1,384,1024]{2,1,0:T(8,128)(2,1)} %param.16) | copy-start | bytes 2359300
  41.6 4.3 %collective-permute-start = (f32[4,16,4,224]{3,1,2,0:T(8,128)S(1)}, f32[4,16,4,224]{3,1,2,0:T(8,128)S(1)}, u32[]{:S(2)}, u32[]{:S(2)}) collective-permute-start(f32[4,16,4,224]{3,1,2,0:T(8,128)S(1)} %bitcast.160), channel_id=1, source_target_pairs={{0,16},{16,0},{1,17},{17,1},{2,18},{18,2},{3,19},{19,3},{4,20},{20... | collective-permute-start | bytes 688136 | tf_op jit(solution)/shard_map/ppermute | solution.py:81
  46.7 17.9 %all-to-all-start.1 = ((f32[16,16,224]{2,1,0:T(8,128)}), f32[16,16,224]{2,1,0:T(8,128)S(1)}, u32[]{:S(2)}, u32[]{:S(2)}) async-start(f32[16,16,224]{2,1,0:T(8,128)} %bitcast.6), calls=%async_computation.1 | async-start | bytes 524288 | tf_op jit(solution)/shard_map/all_to_all | solution.py:83
  65.2 13.2 %all-to-all-start.2 = ((f32[16,1,224]{2,1,0:T(1,128)}), f32[16,1,224]{2,1,0:T(1,128)S(1)}, u32[]{:S(2)}, u32[]{:S(2)}) async-start(f32[16,1,224]{2,1,0:T(1,128)} %reshape_add_fusion), calls=%async_computation.2 | async-start | bytes 32768 | tf_op jit(solution)/shard_map/all_to_all | solution.py:88
  119.1 1.2 copy-start.4
  120.4 1.2 copy-start.2
  122.3 3.3 %collective-permute-start.1 = (f32[4,4,22,128]{3,1,0,2:T(4,128)S(1)}, f32[4,4,22,128]{3,1,0,2:T(4,128)S(1)}, u32[]{:S(2)}, u32[]{:S(2)}) collective-permute-start(f32[4,4,22,128]{3,1,0,2:T(4,128)S(1)} %copy.256), channel_id=1, source_target_pairs={{0,16},{16,0},{1,17},{17,1},{2,18},{18,2},{3,19},{19,3},{4,20},{20... | collective-permute-start | bytes 540680 | tf_op jit(solution)/shard_map/ppermute | solution.py:191
  126.9 17.4 %all-to-all-start.3 = ((f32[16,22,128]{2,1,0:T(8,128)}), f32[16,22,128]{2,1,0:T(8,128)S(1)}, u32[]{:S(2)}, u32[]{:S(2)}) async-start(f32[16,22,128]{2,1,0:T(8,128)} %copy.259), calls=%async_computation.3 | async-start | bytes 393216 | tf_op jit(solution)/shard_map/all_to_all | solution.py:216
  144.4 29.8 %copy-start.1 = (bf16[5120,160]{0,1:T(8,128)(2,1)S(1)}, bf16[5120,160]{0,1:T(8,128)(2,1)}, u32[]{:S(2)}) copy-start(bf16[5120,160]{0,1:T(8,128)(2,1)} %reshape.341) | copy-start | bytes 4915204
  146.2 27.8 %all-to-all-start.4 = ((bf16[32,20,128]{2,1,0:T(8,128)(2,1)}), bf16[32,20,128]{2,1,0:T(8,128)(2,1)S(1)}, u32[]{:S(2)}, u32[]{:S(2)}) async-start(bf16[32,20,128]{2,1,0:T(8,128)(2,1)} %broadcast_in_dim.111), calls=%async_computation.4 | async-start | bytes 393216 | tf_op jit(solution)/shard_map/all_to_all | solution.py:236
Sparse Core Ops, SparseCore 0:
  29.6 59.8 all-gather.3
where the time goes:
time: 183 us; the launch traced here: 182 us
  waiting for transfers between devices  54.9 us (30%)
  starting transfers between devices  45.7 us (25%)
  blocking collectives  38.2 us (21%)
  between operations  15.2 us (8%)
  local copies, waits for them, and re-layouts  14.3 us (8%)
  other arithmetic  7.77 us (4%)
  matrix products  6.08 us (3%)
    all_gather x1, blocking collectives, body(): gathered = lax.all_gather(owned_rows, SEQ, axis=0, tiled=False)  38.2 us
    all_to_all x1, waiting for transfers between devices, body(): lax.all_to_all(jnp.broadcast_to(attention_slice[None], (seq_count,) + att...  17.2 us
    all_to_all x1, starting transfers between devices, body(): lax.all_to_all(jnp.broadcast_to(local_squares[None], (seq_count,) + local...  16.7 us
    all_to_all x1, waiting for transfers between devices, body(): reduced = jnp.sum(lax.all_to_all(chunks, 'z', 0, 0, tiled=True), axis=0)  14.1 us
    all_to_all x1, waiting for transfers between devices, body(): lax.all_to_all(jnp.broadcast_to(local_squares[None], (seq_count,) + local...  10.7 us
    all_to_all x1, starting transfers between devices, body(): lax.all_to_all(jnp.broadcast_to(attention_slice[None], (seq_count,) + att...  9.18 us
    all_to_all x1, waiting for transfers between devices, body(): arrived = lax.all_to_all(pair_packed, 'z', 0, 0, tiled=True)  6.78 us
    all_to_all x1, starting transfers between devices, body(): owned_rows = lax.all_to_all(reduced, 'tensor', 0, 0, tiled=True)  6.76 us
  transfers between devices with their start and end apart: 8, of which 7 were waited for; matrix products, arithmetic and copies ran while one was open for 12% of the time, Pallas kernels for 0%

commit v1 on v0

--- a/solution.py
+++ b/solution.py
@@ -11,6 +11,18 @@
 SEQ = ("z", "core")
 epsilon = 1e-06
 masked_fill = -1e30
+
+
+def _track_forms(panel, on_dim, x_in):
+    far_arr = panel.shape
+    even = panel.reshape(*far_arr[:on_dim], x_in, far_arr[on_dim] // x_in, *far_arr[on_dim + 1 :])
+    return jnp.moveaxis(even, on_dim, 0)
+
+
+def fix_page_in(inputs, row_dim):
+    inputs = jnp.moveaxis(inputs, 0, row_dim)
+    now = inputs.shape
+    return inputs.reshape(*now[:row_dim], now[row_dim] * now[row_dim + 1], *now[row_dim + 2 :])
 
 
 def apply_rotary(values, token_positions):
@@ -40,6 +52,23 @@
     prefix_lens,
     suffix_lens,
 ):
+
+    def targets_save(named_axis, chunk, m, frame_in):
+        u1 = lax.psum(1, axis_name=named_axis)
+        y_new = lax.axis_index(named_axis)
+        later, high = (u1, y_new)
+        frame_out = _track_forms(chunk, frame_in, later)
+        by_rank = [frame_out[high]]
+        for hop_no in range(1, later):
+            odd = frame_out[high ^ hop_no]
+            latest = lax.ppermute(
+                odd, axis_name=named_axis, perm=[(s, s ^ hop_no) for s in range(later)]
+            )
+            by_rank.append(latest)
+        big = jnp.stack(by_rank)
+        frame_out = big[high ^ jnp.arange(later)]
+        return fix_page_in(frame_out, m)
+
     seq_count = lax.axis_size(SEQ)
     tensor_count = lax.axis_size("tensor")
     steps = hidden.shape[0]
@@ -85,7 +114,7 @@
         b_qkv.astype(jnp.float32), seq_index % halves * half_width, half_width
     )
     reduced = reduced + bias[None, :]
-    owned_rows = lax.all_to_all(reduced, "tensor", 0, 0, tiled=True)
+    owned_rows = targets_save("tensor", reduced, 0, 0)
     gathered = lax.all_gather(owned_rows, SEQ, axis=0, tiled=False)
     combined_output = (
         gathered.reshape(steps, requests, halves, tensor_count, half_width)

time: 183 us -> 234 us (1.28)
  starting transfers between devices: 45.7 us -> 94.9 us
  waiting for transfers between devices: 54.9 us -> 51 us
  blocking collectives: 38.2 us -> 41.5 us
    ppermute x0 -> x15, starting transfers between devices: none -> 55.9 us  [targets_save(): lax.ppermute(odd, axis_name=named_axis, perm=[(s, s ^ hop_no) for s in ra...]
    all_to_all x1 -> x0, starting transfers between devices: 6.76 us -> none  [body(): owned_rows = lax.all_to_all(reduced, 'tensor', 0, 0, tiled=True)]
    all_to_all x1 -> x0, waiting for transfers between devices: 3.98 us -> none  [body(): owned_rows = lax.all_to_all(reduced, 'tensor', 0, 0, tiled=True)]
    all_gather x1, blocking collectives: 38.2 us -> 41.5 us  [body(): gathered = lax.all_gather(owned_rows, SEQ, axis=0, tiled=False)]
  transfers between devices with their start and end apart: 8 -> 22, of which waited for: 7 -> 6; matrix products, arithmetic and copies ran while one was open for 12% -> 10% of each run, Pallas kernels for 0% -> 0%
where the time goes in v1:
time: 234 us; the launch traced here: 232 us
  starting transfers between devices  94.9 us (41%)
  waiting for transfers between devices  51 us (22%)
  blocking collectives  41.5 us (18%)
  local copies, waits for them, and re-layouts  15.9 us (7%)
  between operations  15.6 us (7%)
  other arithmetic  7.41 us (3%)
  matrix products  6.04 us (3%)
    ppermute x15, starting transfers between devices, targets_save(): lax.ppermute(odd, axis_name=named_axis, perm=[(s, s ^ hop_no) for s in ra...  55.9 us
    all_gather x1, blocking collectives, body(): gathered = lax.all_gather(owned_rows, SEQ, axis=0, tiled=False)  41.5 us
    all_to_all x1, waiting for transfers between devices, body(): lax.all_to_all(jnp.broadcast_to(attention_slice[None], (seq_count,) + att...  17.9 us
    all_to_all x1, starting transfers between devices, body(): lax.all_to_all(jnp.broadcast_to(local_squares[None], (seq_count,) + local...  16.7 us
    all_to_all x1, waiting for transfers between devices, body(): reduced = jnp.sum(lax.all_to_all(chunks, 'z', 0, 0, tiled=True), axis=0)  14.1 us
    all_to_all x1, waiting for transfers between devices, body(): lax.all_to_all(jnp.broadcast_to(local_squares[None], (seq_count,) + local...  9.98 us
    all_to_all x1, starting transfers between devices, body(): lax.all_to_all(jnp.broadcast_to(attention_slice[None], (seq_count,) + att...  9.18 us
    all_to_all x1, waiting for transfers between devices, body(): arrived = lax.all_to_all(pair_packed, 'z', 0, 0, tiled=True)  6.82 us
  transfers between devices with their start and end apart: 22, of which 6 were waited for; matrix products, arithmetic and copies ran while one was open for 10% of the time, Pallas kernels for 0%

profile of v1, /device:TPU:1, one launch (start us, length us, event | category | flops | bytes accessed | tf_op | source)
XLA Modules:
  0.0 232.2 jit_solution(8645321821641879907)
XLA Ops:
  9.0 16.7 %all-to-all-start = ((f32[32,1,256]{2,1,0:T(1,128)}), f32[32,1,256]{2,1,0:T(1,128)S(1)}, u32[]{:S(2)}, u32[]{:S(2)}) async-start(f32[32,1,256]{2,1,0:T(1,128)} %reshape.377), calls=%async_computation | async-start | bytes 65536 | tf_op jit(solution)/shard_map/all_to_all | solution.py:89
  27.9 10.0 %all-to-all-done = f32[32,1,256]{2,1,0:T(1,128)S(1)} async-done(((f32[32,1,256]{2,1,0:T(1,128)}), f32[32,1,256]{2,1,0:T(1,128)S(1)}, u32[]{:S(2)}, u32[]{:S(2)}) %all-to-all-start) | async-done | bytes 32800 | tf_op jit(solution)/shard_map/all_to_all | solution.py:89
  41.6 3.2 %collective-permute-start = (f32[4,16,4,224]{3,1,2,0:T(8,128)S(1)}, f32[4,16,4,224]{3,1,2,0:T(8,128)S(1)}, u32[]{:S(2)}, u32[]{:S(2)}) collective-permute-start(f32[4,16,4,224]{3,1,2,0:T(8,128)S(1)} %bitcast.186), channel_id=1, source_target_pairs={{0,16},{16,0},{1,17},{17,1},{2,18},{18,2},{3,19},{19,3},{4,20},{20... | collective-permute-start | bytes 688136 | tf_op jit(solution)/shard_map/ppermute | solution.py:110
  46.7 3.5 %all-to-all-start.1 = ((f32[16,16,224]{2,1,0:T(8,128)}), f32[16,16,224]{2,1,0:T(8,128)S(1)}, u32[]{:S(2)}, u32[]{:S(2)}) async-start(f32[16,16,224]{2,1,0:T(8,128)} %bitcast.6), calls=%async_computation.1 | async-start | bytes 524288 | tf_op jit(solution)/shard_map/all_to_all | solution.py:112
  50.5 14.1 %all-to-all-done.1 = f32[16,16,224]{2,1,0:T(8,128)S(1)} async-done(((f32[16,16,224]{2,1,0:T(8,128)}), f32[16,16,224]{2,1,0:T(8,128)S(1)}, u32[]{:S(2)}, u32[]{:S(2)}) %all-to-all-start.1) | async-done | bytes 229408 | tf_op jit(solution)/shard_map/all_to_all | solution.py:112
  64.7 4.4 %collective-permute-start.3 = (f32[1,224]{1,0:T(1,128)S(1)}, f32[1,224]{1,0:T(1,128)S(1)}, u32[]{:S(2)}, u32[]{:S(2)}) collective-permute-start(f32[1,224]{1,0:T(1,128)S(1)} %get-tuple-element.42), channel_id=1, source_target_pairs={{0,3},{1,2},{2,1},{3,0},{4,7},{5,6},{6,5},{7,4},{8,11},{9,10},{10,... | collective-permute-start | bytes 2696 | tf_op jit(solution)/shard_map/ppermute | solution.py:64
  69.1 3.2 %collective-permute-start.4 = (f32[1,224]{1,0:T(1,128)S(1)}, f32[1,224]{1,0:T(1,128)S(1)}, u32[]{:S(2)}, u32[]{:S(2)}) collective-permute-start(f32[1,224]{1,0:T(1,128)S(1)} %get-tuple-element.41), channel_id=1, source_target_pairs={{0,4},{1,5},{2,6},{3,7},{4,0},{5,1},{6,2},{7,3},{8,12},{9,13},{10,... | collective-permute-start | bytes 2696 | tf_op jit(solution)/shard_map/ppermute | solution.py:64
  74.3 4.2 %collective-permute-start.6 = (f32[1,224]{1,0:T(1,128)S(1)}, f32[1,224]{1,0:T(1,128)S(1)}, u32[]{:S(2)}, u32[]{:S(2)}) collective-permute-start(f32[1,224]{1,0:T(1,128)S(1)} %get-tuple-element.39), channel_id=1, source_target_pairs={{0,6},{1,7},{2,4},{3,5},{4,2},{5,3},{6,0},{7,1},{8,14},{9,15},{10,... | collective-permute-start | bytes 2696 | tf_op jit(solution)/shard_map/ppermute | solution.py:64
  78.5 4.3 %collective-permute-start.7 = (f32[1,224]{1,0:T(1,128)S(1)}, f32[1,224]{1,0:T(1,128)S(1)}, u32[]{:S(2)}, u32[]{:S(2)}) collective-permute-start(f32[1,224]{1,0:T(1,128)S(1)} %get-tuple-element.38), channel_id=1, source_target_pairs={{0,7},{1,6},{2,5},{3,4},{4,3},{5,2},{6,1},{7,0},{8,15},{9,14},{10,... | collective-permute-start | bytes 2696 | tf_op jit(solution)/shard_map/ppermute | solution.py:64
  82.8 4.8 %collective-permute-start.8 = (f32[1,224]{1,0:T(1,128)S(1)}, f32[1,224]{1,0:T(1,128)S(1)}, u32[]{:S(2)}, u32[]{:S(2)}) collective-permute-start(f32[1,224]{1,0:T(1,128)S(1)} %get-tuple-element.37), channel_id=1, source_target_pairs={{0,8},{1,9},{2,10},{3,11},{4,12},{5,13},{6,14},{7,15},{8,0},{9,1},... | collective-permute-start | bytes 2696 | tf_op jit(solution)/shard_map/ppermute | solution.py:64
  89.6 5.7 %collective-permute-start.10 = (f32[1,224]{1,0:T(1,128)S(1)}, f32[1,224]{1,0:T(1,128)S(1)}, u32[]{:S(2)}, u32[]{:S(2)}) collective-permute-start(f32[1,224]{1,0:T(1,128)S(1)} %get-tuple-element.35), channel_id=1, source_target_pairs={{0,10},{1,11},{2,8},{3,9},{4,14},{5,15},{6,12},{7,13},{8,2},{9,3},... | collective-permute-start | bytes 2696 | tf_op jit(solution)/shard_map/ppermute | solution.py:64
  95.3 4.2 %collective-permute-start.11 = (f32[1,224]{1,0:T(1,128)S(1)}, f32[1,224]{1,0:T(1,128)S(1)}, u32[]{:S(2)}, u32[]{:S(2)}) collective-permute-start(f32[1,224]{1,0:T(1,128)S(1)} %get-tuple-element.34), channel_id=1, source_target_pairs={{0,11},{1,10},{2,9},{3,8},{4,15},{5,14},{6,13},{7,12},{8,3},{9,2},... | collective-permute-start | bytes 2696 | tf_op jit(solution)/shard_map/ppermute | solution.py:64
  99.4 4.6 %collective-permute-start.12 = (f32[1,224]{1,0:T(1,128)S(1)}, f32[1,224]{1,0:T(1,128)S(1)}, u32[]{:S(2)}, u32[]{:S(2)}) collective-permute-start(f32[1,224]{1,0:T(1,128)S(1)} %get-tuple-element.33), channel_id=1, source_target_pairs={{0,12},{1,13},{2,14},{3,15},{4,8},{5,9},{6,10},{7,11},{8,4},{9,5},... | collective-permute-start | bytes 2696 | tf_op jit(solution)/shard_map/ppermute | solution.py:64
  106.0 5.4 %collective-permute-start.14 = (f32[1,224]{1,0:T(1,128)S(1)}, f32[1,224]{1,0:T(1,128)S(1)}, u32[]{:S(2)}, u32[]{:S(2)}) collective-permute-start(f32[1,224]{1,0:T(1,128)S(1)} %get-tuple-element.31), channel_id=1, source_target_pairs={{0,14},{1,15},{2,12},{3,13},{4,10},{5,11},{6,8},{7,9},{8,6},{9,7},... | collective-permute-start | bytes 2696 | tf_op jit(solution)/shard_map/ppermute | solution.py:64
  111.4 4.1 %collective-permute-start.15 = (f32[1,224]{1,0:T(1,128)S(1)}, f32[1,224]{1,0:T(1,128)S(1)}, u32[]{:S(2)}, u32[]{:S(2)}) collective-permute-start(f32[1,224]{1,0:T(1,128)S(1)} %get-tuple-element.30), channel_id=1, source_target_pairs={{0,15},{1,14},{2,13},{3,12},{4,11},{5,10},{6,9},{7,8},{8,7},{9,6},... | collective-permute-start | bytes 2696 | tf_op jit(solution)/shard_map/ppermute | solution.py:64
  117.5 3.4 %collective-permute-start.2 = (f32[1,224]{1,0:T(1,128)S(1)}, f32[1,224]{1,0:T(1,128)S(1)}, u32[]{:S(2)}, u32[]{:S(2)}) collective-permute-start(f32[1,224]{1,0:T(1,128)S(1)} %get-tuple-element.43), channel_id=1, source_target_pairs={{0,2},{1,3},{2,0},{3,1},{4,6},{5,7},{6,4},{7,5},{8,10},{9,11},{10,... | collective-permute-start | bytes 2696 | tf_op jit(solution)/shard_map/ppermute | solution.py:64
  121.1 2.2 copy.239
  124.0 41.5 %all-gather = f32[512,224]{1,0:T(8,128)S(1)} all-gather(f32[16,224]{1,0:T(8,128)S(1)} %gather_fusion), channel_id=2, replica_groups=mesh['z'=16,'core'=2,'tensor'=16] {'z','core'}, dimensions={0}, use_global_device_ids=true | all-gather | bytes 473088 | tf_op jit(solution)/shard_map/all_gather | solution.py:118
  176.9 4.2 %all-to-all-start.2 = ((f32[16,22,128]{2,1,0:T(8,128)}), f32[16,22,128]{2,1,0:T(8,128)S(1)}, u32[]{:S(2)}, u32[]{:S(2)}) async-start(f32[16,22,128]{2,1,0:T(8,128)} %copy.212), calls=%async_computation.2 | async-start | bytes 393216 | tf_op jit(solution)/shard_map/all_to_all | solution.py:245
  182.7 2.2 copy.182
  184.9 2.6 %reshape.372 = bf16[5120,160]{0,1:T(8,128)(2,1)} reshape(bf16[16,320,160]{1,0,2:T(8,128)(2,1)S(1)} %copy.182) | data formatting | bytes 3276800 | tf_op jit(solution)/shard_map/optimization_barrier | solution.py:246
  187.5 6.8 %all-to-all-done.2 = f32[16,22,128]{2,1,0:T(8,128)S(1)} async-done(((f32[16,22,128]{2,1,0:T(8,128)}), f32[16,22,128]{2,1,0:T(8,128)S(1)}, u32[]{:S(2)}, u32[]{:S(2)}) %all-to-all-start.2) | async-done | bytes 180256 | tf_op jit(solution)/shard_map/all_to_all | solution.py:245
  196.2 9.2 %all-to-all-start.3 = ((bf16[32,20,128]{2,1,0:T(8,128)(2,1)}), bf16[32,20,128]{2,1,0:T(8,128)(2,1)S(1)}, u32[]{:S(2)}, u32[]{:S(2)}) async-start(bf16[32,20,128]{2,1,0:T(8,128)(2,1)} %broadcast_in_dim.112), calls=%async_computation.3 | async-start | bytes 393216 | tf_op jit(solution)/shard_map/all_to_all | solution.py:265
  206.1 17.9 %all-to-all-done.3 = bf16[32,20,128]{2,1,0:T(8,128)(2,1)S(1)} async-done(((bf16[32,20,128]{2,1,0:T(8,128)(2,1)}), bf16[32,20,128]{2,1,0:T(8,128)(2,1)S(1)}, u32[]{:S(2)}, u32[]{:S(2)}) %all-to-all-start.3) | async-done | bytes 163872 | tf_op jit(solution)/shard_map/all_to_all | solution.py:265
  (123 shorter events, 34.3 us)
Async XLA Ops:
  7.2 161.3 %copy-start = (bf16[4,128,1024]{2,1,0:T(8,128)(2,1)S(1)}, bf16[4,128,1024]{2,1,0:T(8,128)(2,1)}, u32[]{:S(2)}) copy-start(bf16[4,128,1024]{2,1,0:T(8,128)(2,1)} %param.18) | copy-start | bytes 3145732
  9.0 28.9 %all-to-all-start = ((f32[32,1,256]{2,1,0:T(1,128)}), f32[32,1,256]{2,1,0:T(1,128)S(1)}, u32[]{:S(2)}, u32[]{:S(2)}) async-start(f32[32,1,256]{2,1,0:T(1,128)} %reshape.377), calls=%async_computation | async-start | bytes 65536 | tf_op jit(solution)/shard_map/all_to_all | solution.py:89
  25.8 156.9 %all-gather.4.cloned.1.call-start = ((), (), s32[]{:S(2)}) async-start(), calls=%async_computation.4 | async-start | bytes 2088960 | tf_op jit(solution)/shard_map/all_gather | solution.py:85
  41.5 79.4 %copy-start.3 = (bf16[1,384,1024]{2,1,0:T(8,128)(2,1)S(1)}, bf16[1,384,1024]{2,1,0:T(8,128)(2,1)}, u32[]{:S(2)}) copy-start(bf16[1,384,1024]{2,1,0:T(8,128)(2,1)} %param.16) | copy-start | bytes 2359300
  41.6 4.3 %collective-permute-start = (f32[4,16,4,224]{3,1,2,0:T(8,128)S(1)}, f32[4,16,4,224]{3,1,2,0:T(8,128)S(1)}, u32[]{:S(2)}, u32[]{:S(2)}) collective-permute-start(f32[4,16,4,224]{3,1,2,0:T(8,128)S(1)} %bitcast.186), channel_id=1, source_target_pairs={{0,16},{16,0},{1,17},{17,1},{2,18},{18,2},{3,19},{19,3},{4,20},{20... | collective-permute-start | bytes 688136 | tf_op jit(solution)/shard_map/ppermute | solution.py:110
  46.7 17.9 %all-to-all-start.1 = ((f32[16,16,224]{2,1,0:T(8,128)}), f32[16,16,224]{2,1,0:T(8,128)S(1)}, u32[]{:S(2)}, u32[]{:S(2)}) async-start(f32[16,16,224]{2,1,0:T(8,128)} %bitcast.6), calls=%async_computation.1 | async-start | bytes 524288 | tf_op jit(solution)/shard_map/all_to_all | solution.py:112
  64.7 18.0 %collective-permute-start.3 = (f32[1,224]{1,0:T(1,128)S(1)}, f32[1,224]{1,0:T(1,128)S(1)}, u32[]{:S(2)}, u32[]{:S(2)}) collective-permute-start(f32[1,224]{1,0:T(1,128)S(1)} %get-tuple-element.42), channel_id=1, source_target_pairs={{0,3},{1,2},{2,1},{3,0},{4,7},{5,6},{6,5},{7,4},{8,11},{9,10},{10,... | collective-permute-start | bytes 2696 | tf_op jit(solution)/shard_map/ppermute | solution.py:64
  69.1 18.5 %collective-permute-start.4 = (f32[1,224]{1,0:T(1,128)S(1)}, f32[1,224]{1,0:T(1,128)S(1)}, u32[]{:S(2)}, u32[]{:S(2)}) collective-permute-start(f32[1,224]{1,0:T(1,128)S(1)} %get-tuple-element.41), channel_id=1, source_target_pairs={{0,4},{1,5},{2,6},{3,7},{4,0},{5,1},{6,2},{7,3},{8,12},{9,13},{10,... | collective-permute-start | bytes 2696 | tf_op jit(solution)/shard_map/ppermute | solution.py:64
  72.4 17.2 %collective-permute-start.5 = (f32[1,224]{1,0:T(1,128)S(1)}, f32[1,224]{1,0:T(1,128)S(1)}, u32[]{:S(2)}, u32[]{:S(2)}) collective-permute-start(f32[1,224]{1,0:T(1,128)S(1)} %get-tuple-element.40), channel_id=1, source_target_pairs={{0,5},{1,4},{2,7},{3,6},{4,1},{5,0},{6,3},{7,2},{8,13},{9,12},{10,... | collective-permute-start | bytes 2696 | tf_op jit(solution)/shard_map/ppermute | solution.py:64
  74.3 21.0 %collective-permute-start.6 = (f32[1,224]{1,0:T(1,128)S(1)}, f32[1,224]{1,0:T(1,128)S(1)}, u32[]{:S(2)}, u32[]{:S(2)}) collective-permute-start(f32[1,224]{1,0:T(1,128)S(1)} %get-tuple-element.39), channel_id=1, source_target_pairs={{0,6},{1,7},{2,4},{3,5},{4,2},{5,3},{6,0},{7,1},{8,14},{9,15},{10,... | collective-permute-start | bytes 2696 | tf_op jit(solution)/shard_map/ppermute | solution.py:64
  78.5 21.0 %collective-permute-start.7 = (f32[1,224]{1,0:T(1,128)S(1)}, f32[1,224]{1,0:T(1,128)S(1)}, u32[]{:S(2)}, u32[]{:S(2)}) collective-permute-start(f32[1,224]{1,0:T(1,128)S(1)} %get-tuple-element.38), channel_id=1, source_target_pairs={{0,7},{1,6},{2,5},{3,4},{4,3},{5,2},{6,1},{7,0},{8,15},{9,14},{10,... | collective-permute-start | bytes 2696 | tf_op jit(solution)/shard_map/ppermute | solution.py:64
  82.8 21.3 %collective-permute-start.8 = (f32[1,224]{1,0:T(1,128)S(1)}, f32[1,224]{1,0:T(1,128)S(1)}, u32[]{:S(2)}, u32[]{:S(2)}) collective-permute-start(f32[1,224]{1,0:T(1,128)S(1)} %get-tuple-element.37), channel_id=1, source_target_pairs={{0,8},{1,9},{2,10},{3,11},{4,12},{5,13},{6,14},{7,15},{8,0},{9,1},... | collective-permute-start | bytes 2696 | tf_op jit(solution)/shard_map/ppermute | solution.py:64
  87.6 18.4 %collective-permute-start.9 = (f32[1,224]{1,0:T(1,128)S(1)}, f32[1,224]{1,0:T(1,128)S(1)}, u32[]{:S(2)}, u32[]{:S(2)}) collective-permute-start(f32[1,224]{1,0:T(1,128)S(1)} %get-tuple-element.36), channel_id=1, source_target_pairs={{0,9},{1,8},{2,11},{3,10},{4,13},{5,12},{6,15},{7,14},{8,1},{9,0},... | collective-permute-start | bytes 2696 | tf_op jit(solution)/shard_map/ppermute | solution.py:64
  89.6 21.9 %collective-permute-start.10 = (f32[1,224]{1,0:T(1,128)S(1)}, f32[1,224]{1,0:T(1,128)S(1)}, u32[]{:S(2)}, u32[]{:S(2)}) collective-permute-start(f32[1,224]{1,0:T(1,128)S(1)} %get-tuple-element.35), channel_id=1, source_target_pairs={{0,10},{1,11},{2,8},{3,9},{4,14},{5,15},{6,12},{7,13},{8,2},{9,3},... | collective-permute-start | bytes 2696 | tf_op jit(solution)/shard_map/ppermute | solution.py:64
  95.3 20.3 %collective-permute-start.11 = (f32[1,224]{1,0:T(1,128)S(1)}, f32[1,224]{1,0:T(1,128)S(1)}, u32[]{:S(2)}, u32[]{:S(2)}) collective-permute-start(f32[1,224]{1,0:T(1,128)S(1)} %get-tuple-element.34), channel_id=1, source_target_pairs={{0,11},{1,10},{2,9},{3,8},{4,15},{5,14},{6,13},{7,12},{8,3},{9,2},... | collective-permute-start | bytes 2696 | tf_op jit(solution)/shard_map/ppermute | solution.py:64
  99.4 18.1 %collective-permute-start.12 = (f32[1,224]{1,0:T(1,128)S(1)}, f32[1,224]{1,0:T(1,128)S(1)}, u32[]{:S(2)}, u32[]{:S(2)}) collective-permute-start(f32[1,224]{1,0:T(1,128)S(1)} %get-tuple-element.33), channel_id=1, source_target_pairs={{0,12},{1,13},{2,14},{3,15},{4,8},{5,9},{6,10},{7,11},{8,4},{9,5},... | collective-permute-start | bytes 2696 | tf_op jit(solution)/shard_map/ppermute | solution.py:64
  104.1 19.2 %collective-permute-start.13 = (f32[1,224]{1,0:T(1,128)S(1)}, f32[1,224]{1,0:T(1,128)S(1)}, u32[]{:S(2)}, u32[]{:S(2)}) collective-permute-start(f32[1,224]{1,0:T(1,128)S(1)} %get-tuple-element.32), channel_id=1, source_target_pairs={{0,13},{1,12},{2,15},{3,14},{4,9},{5,8},{6,11},{7,10},{8,5},{9,4},... | collective-permute-start | bytes 2696 | tf_op jit(solution)/shard_map/ppermute | solution.py:64
  106.0 17.3 %collective-permute-start.14 = (f32[1,224]{1,0:T(1,128)S(1)}, f32[1,224]{1,0:T(1,128)S(1)}, u32[]{:S(2)}, u32[]{:S(2)}) collective-permute-start(f32[1,224]{1,0:T(1,128)S(1)} %get-tuple-element.31), channel_id=1, source_target_pairs={{0,14},{1,15},{2,12},{3,13},{4,10},{5,11},{6,8},{7,9},{8,6},{9,7},... | collective-permute-start | bytes 2696 | tf_op jit(solution)/shard_map/ppermute | solution.py:64
  111.4 11.9 %collective-permute-start.15 = (f32[1,224]{1,0:T(1,128)S(1)}, f32[1,224]{1,0:T(1,128)S(1)}, u32[]{:S(2)}, u32[]{:S(2)}) collective-permute-start(f32[1,224]{1,0:T(1,128)S(1)} %get-tuple-element.30), channel_id=1, source_target_pairs={{0,15},{1,14},{2,13},{3,12},{4,11},{5,10},{6,9},{7,8},{8,7},{9,6},... | collective-permute-start | bytes 2696 | tf_op jit(solution)/shard_map/ppermute | solution.py:64
  115.6 7.8 %collective-permute-start.1 = (f32[1,224]{1,0:T(1,128)S(1)}, f32[1,224]{1,0:T(1,128)S(1)}, u32[]{:S(2)}, u32[]{:S(2)}) collective-permute-start(f32[1,224]{1,0:T(1,128)S(1)} %get-tuple-element.44), channel_id=1, source_target_pairs={{0,1},{1,0},{2,3},{3,2},{4,5},{5,4},{6,7},{7,6},{8,9},{9,8},{10,11... | collective-permute-start | bytes 2696 | tf_op jit(solution)/shard_map/ppermute | solution.py:64
  117.5 5.8 %collective-permute-start.2 = (f32[1,224]{1,0:T(1,128)S(1)}, f32[1,224]{1,0:T(1,128)S(1)}, u32[]{:S(2)}, u32[]{:S(2)}) collective-permute-start(f32[1,224]{1,0:T(1,128)S(1)} %get-tuple-element.43), channel_id=1, source_target_pairs={{0,2},{1,3},{2,0},{3,1},{4,6},{5,7},{6,4},{7,5},{8,10},{9,11},{10,... | collective-permute-start | bytes 2696 | tf_op jit(solution)/shard_map/ppermute | solution.py:64
  172.3 3.3 %collective-permute-start.16 = (f32[4,4,22,128]{3,1,0,2:T(4,128)S(1)}, f32[4,4,22,128]{3,1,0,2:T(4,128)S(1)}, u32[]{:S(2)}, u32[]{:S(2)}) collective-permute-start(f32[4,4,22,128]{3,1,0,2:T(4,128)S(1)} %copy.209), channel_id=1, source_target_pairs={{0,16},{16,0},{1,17},{17,1},{2,18},{18,2},{3,19},{19,3},{4,20},{20... | collective-permute-start | bytes 540680 | tf_op jit(solution)/shard_map/ppermute | solution.py:220
  176.9 17.4 %all-to-all-start.2 = ((f32[16,22,128]{2,1,0:T(8,128)}), f32[16,22,128]{2,1,0:T(8,128)S(1)}, u32[]{:S(2)}, u32[]{:S(2)}) async-start(f32[16,22,128]{2,1,0:T(8,128)} %copy.212), calls=%async_computation.2 | async-start | bytes 393216 | tf_op jit(solution)/shard_map/all_to_all | solution.py:245
  196.2 27.8 %all-to-all-start.3 = ((bf16[32,20,128]{2,1,0:T(8,128)(2,1)}), bf16[32,20,128]{2,1,0:T(8,128)(2,1)S(1)}, u32[]{:S(2)}, u32[]{:S(2)}) async-start(bf16[32,20,128]{2,1,0:T(8,128)(2,1)} %broadcast_in_dim.112), calls=%async_computation.3 | async-start | bytes 393216 | tf_op jit(solution)/shard_map/all_to_all | solution.py:265
  (5 other events, 45.3 us)
Sparse Core Ops, SparseCore 0:
  29.6 59.8 all-gather.3
